TPU v7x, 256 devices: a whole 4x4x8 slice. The times are simulated.
256 devices in a mesh: section: 2 (over core), seq: 16 (over x, y), exp: 8 (over z).
Axes of the slice: x: 4, y: 4, z: 8, core: 2. Of those that a mesh axis runs over, the one named last changes fastest.
Arguments:
- hidden_in: bfloat16 [2048, 2048], P('seq'), may hold values from -6 to 6
- seg_ids: int32 [2048], P('seq'), may hold values from 0 to 7, never falling along the last dimension, each value on 1 to 1024 neighbouring positions
- attn_gain: float32 [2048], replicated, may hold values from 0.25 to 1.75
- w_query: bfloat16 [2048, 2048], P(None, ('section', 'exp'))
- w_key: bfloat16 [2048, 2048], P(None, ('section', 'exp'))
- w_value: bfloat16 [2048, 2048], P(None, ('section', 'exp')), may hold values from -0.125 to 0.125
- w_out: bfloat16 [2048, 2048], P(('section', 'exp')), may hold values from -0.5 to 0.5
- moe_gain: float32 [2048], replicated, may hold values from 0.25 to 1.75
- expert_ids: int32 [2048, 8], P(('seq', 'exp')), may hold values from 0 to 63, all different within a row; in each aligned block of 16 rows (0 to 15, 16 to 31, ...) at most 4 rows name the same one
- route_weights: float32 [2048, 8], P(('seq', 'exp')), may hold values from 0.1 to 0.6
- gate_halves: bfloat16 [128, 2048, 512], P(('seq', 'exp'), None, 'section'), may hold values from -0.125 to 0.125
- up_halves: bfloat16 [128, 2048, 512], P(('seq', 'exp'), None, 'section'), may hold values from -0.125 to 0.125
- down_halves: bfloat16 [128, 512, 2048], P(('seq', 'exp'), 'section'), may hold values from -0.1875 to 0.1875
Outputs:
- layer_out: bfloat16 [2048, 2048], P(('seq', 'exp'))
Inputs may be any that keep to these rules, and one draw needn't show every extreme that they name: `seg_ids`: prompt numbers never fall along the batch; each prompt holds 1 to 1024 tokens, and one holds exactly 1024. `expert_ids`: A token's 8 experts are distinct. In each aligned block of 16 tokens (the tokens of one device along seq and exp), no expert is chosen by more than 4 of the block's tokens, a bound that some block reaches.
All inputs are finite; a program needn't handle non-finite values.
Results may differ from a plain program's by a relative error of at most 0.012.
Values may be sent and summed in bfloat16 or wider, within the bound.
No kernel may reach another device: no remote copies, remote signals or barrier semaphores. Data moves between devices by JAX's collectives and lax.ppermute only.
A program may use at most 64 MiB of HBM per device.

v0:
```python
import math
import jax
import jax.numpy as jnp
from jax import lax
from jax.sharding import PartitionSpec as P

epsilon = 1e-05
rope_base = 10000.0


def rms_scale(rows, gain):
    wide = rows.astype(jnp.float32)
    inverse = lax.rsqrt(jnp.mean(wide * wide, axis=-1, keepdims=True) + epsilon)
    return (wide * inverse * gain).astype(jnp.bfloat16)


def rotate(values, positions):
    half_dim = values.shape[-1] // 2
    frequency = rope_base ** (-2.0 * jnp.arange(half_dim, dtype=jnp.float32) / values.shape[-1])
    angles = positions.astype(jnp.float32)[:, None] * frequency[None, :]
    cosine = jnp.cos(angles)
    sine_part = jnp.sin(angles)
    first_half = values[:, :half_dim]
    second_half = values[:, half_dim:]
    return jnp.concatenate(
        [
            first_half * cosine - second_half * sine_part,
            second_half * cosine + first_half * sine_part,
        ],
        axis=-1,
    )


def per_device(
    hidden_in,
    seg_ids,
    attn_gain,
    w_query,
    w_key,
    w_value,
    w_out,
    moe_gain,
    expert_ids,
    route_weights,
    gate_halves,
    up_halves,
    down_halves,
):
    tok_seq = hidden_in.shape[0]
    width = hidden_in.shape[1]
    head_dim = w_query.shape[1]
    positions = lax.axis_index("seq") * tok_seq + jnp.arange(tok_seq, dtype=jnp.int32)
    normed = rms_scale(hidden_in, attn_gain)
    query_rows = rotate(
        jnp.dot(normed, w_query, preferred_element_type=jnp.float32), positions
    ).astype(jnp.bfloat16)
    key_rows = rotate(jnp.dot(normed, w_key, preferred_element_type=jnp.float32), positions).astype(
        jnp.bfloat16
    )
    value_rows = jnp.dot(normed, w_value, preferred_element_type=jnp.float32).astype(jnp.bfloat16)
    score_scale = 1.0 / math.sqrt(head_dim)
    run_max = jnp.full((tok_seq,), -1e30, jnp.float32)
    piece_keys = lax.all_gather(key_rows, "seq", axis=0, tiled=True)
    piece_values = lax.all_gather(value_rows, "seq", axis=0, tiled=True)
    key_segs = lax.all_gather(seg_ids, "seq", axis=0, tiled=True)
    piece_rows = piece_keys.shape[0]
    scores = (
        lax.dot_general(
            query_rows, piece_keys, (((1,), (1,)), ((), ())), preferred_element_type=jnp.float32
        )
        * score_scale
    )
    key_pos = jnp.arange(piece_rows, dtype=jnp.int32)
    allowed = (seg_ids[:, None] == key_segs[None, :]) & (key_pos[None, :] <= positions[:, None])
    masked = jnp.where(allowed, scores, -1e30)
    new_max = jnp.maximum(run_max, jnp.max(masked, axis=1))
    weights = jnp.where(allowed, jnp.exp(masked - new_max[:, None]), 0.0)
    run_total = jnp.sum(weights, axis=1)
    weighted_sum = jnp.dot(
        weights.astype(jnp.bfloat16), piece_values, preferred_element_type=jnp.float32
    )
    run_max, run_total, weighted_sum = (new_max, run_total, weighted_sum)
    head_out = (weighted_sum / run_total[:, None]).astype(jnp.bfloat16)
    partial_value = jnp.dot(head_out, w_out, preferred_element_type=jnp.float32)
    tok_dev = tok_seq // lax.axis_size("exp")
    own_start = lax.axis_index("exp") * tok_dev
    summed = lax.psum(partial_value, ("section", "exp"))
    summed = lax.dynamic_slice_in_dim(summed, own_start, tok_dev, 0)
    own_rows = lax.dynamic_slice_in_dim(hidden_in, own_start, tok_dev, 0)
    residual = (own_rows.astype(jnp.float32) + summed).astype(jnp.bfloat16)
    moe_in = rms_scale(residual, moe_gain)
    experts = lax.axis_size("seq") * lax.axis_size("exp") // 2
    top_count = expert_ids.shape[1]
    capacity = min(tok_dev, max(2, 2 * tok_dev * top_count // experts))
    row_count = tok_dev * top_count
    flat_ids = expert_ids.reshape(row_count)
    one_hot = (flat_ids[:, None] == jnp.arange(experts, dtype=jnp.int32)[None, :]).astype(jnp.int32)
    slot_rank = jnp.sum((jnp.cumsum(one_hot, axis=0) - one_hot) * one_hot, axis=1)
    slot_index = flat_ids * capacity + slot_rank
    placed = slot_index[:, None] == jnp.arange(experts * capacity, dtype=jnp.int32)[None, :]
    repeated = jnp.repeat(moe_in, top_count, axis=0)
    outgoing = lax.dot_general(
        placed.astype(jnp.bfloat16),
        repeated,
        (((0,), (0,)), ((), ())),
        preferred_element_type=jnp.float32,
    ).astype(jnp.bfloat16)
    row_token = jnp.arange(row_count, dtype=jnp.int32) // top_count
    token_hot = (row_token[None, :] == jnp.arange(tok_dev, dtype=jnp.int32)[:, None]).astype(
        jnp.float32
    )
    weighted = token_hot * route_weights.reshape(row_count)[None, :]
    combine = jnp.dot(weighted, placed.astype(jnp.float32), precision=lax.Precision.HIGHEST)
    doubled = jnp.broadcast_to(
        outgoing.reshape(experts, 1, capacity, width), (experts, 2, capacity, width)
    ).reshape(2 * experts, capacity, width)
    arrived = lax.all_to_all(doubled, ("seq", "exp"), split_axis=0, concat_axis=0, tiled=True)
    flat_rows = arrived.reshape(-1, width)
    gate_proj = jnp.dot(flat_rows, gate_halves[0], preferred_element_type=jnp.float32)
    up_proj = jnp.dot(flat_rows, up_halves[0], preferred_element_type=jnp.float32)
    activated = (jax.nn.silu(gate_proj) * up_proj).astype(jnp.bfloat16)
    returned = lax.all_to_all(
        jnp.dot(activated, down_halves[0], preferred_element_type=jnp.float32)
        .astype(jnp.bfloat16)
        .reshape(arrived.shape),
        ("seq", "exp"),
        split_axis=0,
        concat_axis=0,
        tiled=True,
    )
    halves_sum = jnp.sum(
        returned.reshape(experts, 2, capacity, width).astype(jnp.float32), axis=1
    ).reshape(experts * capacity, width)
    moe_part = jnp.dot(combine, halves_sum, precision=lax.Precision.HIGHEST)
    moe_total = lax.psum(moe_part, "section")
    return (residual.astype(jnp.float32) + moe_total).astype(jnp.bfloat16)


def solution(mesh):
    in_specs = (
        P("seq", None),
        P("seq"),
        P(),
        P(None, ("section", "exp")),
        P(None, ("section", "exp")),
        P(None, ("section", "exp")),
        P(("section", "exp"), None),
        P(),
        P(("seq", "exp"), None),
        P(("seq", "exp"), None),
        P(("seq", "exp"), None, "section"),
        P(("seq", "exp"), None, "section"),
        P(("seq", "exp"), "section", None),
    )
    out_specs = P(("seq", "exp"), None)
    return jax.shard_map(
        per_device, mesh=mesh, in_specs=in_specs, out_specs=out_specs, check_vma=False
    )
```

profile of v0, /device:TPU:1, one launch (start us, length us, event | category | flops | bytes accessed | tf_op | source)
XLA Modules:
  0.0 376.0 jit_solution(10940934380651629049)
XLA Ops:
  6.5 0.0 copy-start
  6.5 0.0 all-reduce.3.cloned.1.call-start
  6.6 1.3 fusion.4
  7.9 1.6 fusion.74
  9.5 0.0 copy-start.2
  9.5 0.0 copy-start.7
  9.6 0.0 copy-start.8
  9.6 1.7 fusion.76
  11.3 0.2 fusion.52
  11.5 20.5 %all_gather.10 = bf16[2048,128]{0,1:T(8,128)(2,1)S(1)} all-gather(bf16[128,128]{0,1:T(8,128)(2,1)S(1)} %pad_maximum_fusion), channel_id=1, replica_groups=mesh['section'=2,'seq'=16,'exp'=8] {'seq'}, dimensions={0}, use_global_device_ids=true | all-gather | bytes 557056 | tf_op jit(solution)/shard_map/all_gather | solution.py:63
  32.0 15.7 %all-gather = s32[16,1,128]{2,1,0:T(1,128)S(1)} all-gather(s32[1,1,128]{2,1,0:T(1,128)S(1)} %bitcast.33), channel_id=1, replica_groups=mesh['section'=2,'seq'=16,'exp'=8] {'seq'}, dimensions={0}, use_global_device_ids=true | all-gather | bytes 8704 | tf_op jit(solution)/shard_map/all_gather | solution.py:65
  47.8 0.5 fusion.78
  48.3 0.4 convolution_convert_fusion.2
  48.7 16.1 %all_gather.11 = bf16[2048,128]{1,0:T(8,128)(2,1)S(1)} all-gather(bf16[128,128]{1,0:T(8,128)(2,1)S(1)} %convolution_convert_fusion.2), channel_id=1, replica_groups=mesh['section'=2,'seq'=16,'exp'=8] {'seq'}, dimensions={0}, use_global_device_ids=true | all-gather | bytes 557056 | tf_op jit(solution)/shard_map/all_gather | solution.py:64
  64.8 0.4 fusion.13
  65.2 0.0 copy-start.3
  65.2 2.8 fusion.3
  68.0 0.0 all-reduce.3.cloned.1.call-update
  68.1 0.1 copy.19
  68.1 0.1 reshape.82
  68.2 0.1 fusion.42
  68.3 0.2 reduce_window_sum.11
  68.5 0.2 select_reduce_fusion
  68.7 128.0 %all-reduce.3.cloned.1.call-done = f32[128,2048]{1,0:T(8,128)} async-done(((f32[128,2048]{1,0:T(8,128)}), f32[128,2048]{1,0:T(8,128)}) %all-reduce.3.cloned.1.call-update) | async-done | bytes 1048592 | tf_op jit(solution)/shard_map/psum | solution.py:87
  196.7 1.0 fusion.35
  197.7 0.1 fusion.37
  197.8 0.5 convolution_convert_fusion.1
  198.4 0.4 broadcast_in_dim.19
  198.8 1.2 broadcast_in_dim.20
  200.1 63.0 %all_to_all.10 = bf16[128,4,2048]{2,1,0:T(4,128)(2,1)S(1)} all-to-all(bf16[128,4,2048]{2,1,0:T(4,128)(2,1)S(1)} %bitcast.29), channel_id=1, replica_groups=mesh['section'=2,'seq'=16,'exp'=8] {'seq','exp'}, dimensions={0} | all-to-all | bytes 4194304 | tf_op jit(solution)/shard_map/all_to_all | solution.py:117
  263.1 2.1 reshape.85
  265.1 3.5 fusion.10
  268.7 0.0 copy-done
  268.7 5.0 %convolution_convert_fusion = bf16[512,2048]{1,0:T(8,128)(2,1)} fusion(bf16[512,2048]{1,0:T(8,128)(2,1)S(1)} %copy-done.1, bf16[1,256,2048]{2,1,0:T(8,128)(2,1)S(1)} %copy-done, bf16[1,2048,256]{2,1,0:T(8,128)(2,1)} %param.24, f32[512,256]{1,0:T(8,128)} %fusion.10), kind=kOutput, calls=%fused_computation.1 | convolution fusion | flops 1075576832 | bytes 6815744 | tf_op jit(solution)/shard_map/dot_general | solution.py:123
  273.7 4.1 %reshape.86 = bf16[128,4,2048]{2,1,0:T(4,128)(2,1)} reshape(bf16[512,2048]{1,0:T(8,128)(2,1)} %convolution_convert_fusion) | data formatting | bytes 4194304 | tf_op jit(solution)/shard_map/reshape | solution.py:125
  277.8 6.7 %all-to-all-start.1 = ((bf16[128,4,2048]{2,1,0:T(4,128)(2,1)}), bf16[128,4,2048]{2,1,0:T(4,128)(2,1)S(1)}, u32[]{:S(2)}, u32[]{:S(2)}) async-start(bf16[128,4,2048]{2,1,0:T(4,128)(2,1)} %reshape.86), calls=%async_computation.1 | async-start | bytes 4194304 | tf_op jit(solution)/shard_map/all_to_all | solution.py:122
  284.6 0.2 all-reduce.5.cloned.1.call-start
  284.8 0.0 copy-done.6
  284.8 0.1 copy.18
  284.9 0.1 mul.147
  285.0 0.2 fusion.39
  285.2 49.4 %all-to-all-done.1 = bf16[128,4,2048]{2,1,0:T(4,128)(2,1)S(1)} async-done(((bf16[128,4,2048]{2,1,0:T(4,128)(2,1)}), bf16[128,4,2048]{2,1,0:T(4,128)(2,1)S(1)}, u32[]{:S(2)}, u32[]{:S(2)}) %all-to-all-start.1) | async-done | bytes 2097184 | tf_op jit(solution)/shard_map/all_to_all | solution.py:122
  334.5 2.7 convert_reduce_fusion
  337.2 2.0 reshape.87
  339.2 1.8 fusion.79
  341.0 0.0 all-reduce.5.cloned.1.call-update
  341.0 26.6 %all-reduce.5.cloned.1.call-done = f32[16,2048]{1,0:T(8,128)} async-done(((f32[16,2048]{1,0:T(8,128)}), f32[16,2048]{1,0:T(8,128)}) %all-reduce.5.cloned.1.call-update) | async-done | bytes 131088 | tf_op jit(solution)/shard_map/psum | solution.py:135
  367.6 1.5 fusion.38
  (20 shorter events, 0.1 us)
Async XLA Ops:
  6.5 262.1 %copy-start = (bf16[1,256,2048]{2,1,0:T(8,128)(2,1)S(1)}, bf16[1,256,2048]{2,1,0:T(8,128)(2,1)}, u32[]{:S(2)}) copy-start(bf16[1,256,2048]{2,1,0:T(8,128)(2,1)} %param.25) | copy-start | bytes 3145732
  6.5 25.5 %copy-start.4 = (s32[128]{0:T(128)S(1)}, s32[128]{0:T(128)}, u32[]{:S(2)}) copy-start(s32[128]{0:T(128)} %param.14) | copy-start | bytes 1540
  6.5 190.1 %all-reduce.3.cloned.1.call-start = ((), (), s32[]{:S(2)}) async-start(), calls=%async_computation.2 | async-start | bytes 2097152 | tf_op jit(solution)/shard_map/psum | solution.py:87
  9.5 38.8 %copy-start.2 = (bf16[128,2048]{1,0:T(8,128)(2,1)S(1)}, bf16[128,2048]{1,0:T(8,128)(2,1)}, u32[]{:S(2)}) copy-start(bf16[128,2048]{1,0:T(8,128)(2,1)} %param.13) | copy-start | bytes 1572868
  9.5 38.8 %copy-start.7 = (bf16[2048,128]{1,0:T(8,128)(2,1)S(1)}, bf16[2048,128]{1,0:T(8,128)(2,1)}, u32[]{:S(2)}) copy-start(bf16[2048,128]{1,0:T(8,128)(2,1)} %param.18) | copy-start | bytes 1572868
  9.6 38.8 %copy-start.8 = (f32[2048]{0:T(1024)S(1)}, f32[2048]{0:T(1024)}, u32[]{:S(2)}) copy-start(f32[2048]{0:T(1024)} %param.15) | copy-start | bytes 24580
  65.2 2.8 copy-start.5
  65.2 132.5 %copy-start.3 = (f32[2048]{0:T(1024)S(1)}, f32[2048]{0:T(1024)}, u32[]{:S(2)}) copy-start(f32[2048]{0:T(1024)} %param.20) | copy-start | bytes 24580
  265.1 3.5 copy-start.1
  277.8 7.0 %copy-start.6 = (f32[16,8]{0,1:T(8,128)S(1)}, f32[16,8]{0,1:T(8,128)}, u32[]{:S(2)}) copy-start(f32[16,8]{0,1:T(8,128)} %param.22) | copy-start | bytes 1540
  277.8 56.7 %all-to-all-start.1 = ((bf16[128,4,2048]{2,1,0:T(4,128)(2,1)}), bf16[128,4,2048]{2,1,0:T(4,128)(2,1)S(1)}, u32[]{:S(2)}, u32[]{:S(2)}) async-start(bf16[128,4,2048]{2,1,0:T(4,128)(2,1)} %reshape.86), calls=%async_computation.1 | async-start | bytes 4194304 | tf_op jit(solution)/shard_map/all_to_all | solution.py:122
  284.6 83.1 %all-reduce.5.cloned.1.call-start = ((), (), s32[]{:S(2)}) async-start(), calls=%async_computation.3 | async-start | bytes 262144 | tf_op jit(solution)/shard_map/psum | solution.py:135
Sparse Core Ops, SparseCore 0:
  68.2 128.4 all-reduce.2
  341.1 26.4 all-reduce.4
where the time goes:
time: 377 us; the launch traced here: 376 us
  waiting for transfers between devices  204 us (54%)
  blocking collectives  115 us (31%)
  matrix products  18 us (5%)
  between operations  13.6 us (4%)
  local copies, waits for them, and re-layouts  10.2 us (3%)
  other arithmetic  7.82 us (2%)
  starting transfers between devices  6.96 us (2%)
    psum x1, waiting for transfers between devices, per_device(): summed = lax.psum(partial_value, ('section', 'exp'))  128 us
    all_to_all x1, blocking collectives, per_device(): lax.all_to_all(doubled, ('seq', 'exp'), split_axis=0, concat_axis=0, tile...  63 us
    all_to_all x1, waiting for transfers between devices, per_device(): lax.all_to_all(jnp.dot(activated, down_halves[0], preferred_element_type=...  49.4 us
    psum x1, waiting for transfers between devices, per_device(): moe_total = lax.psum(moe_part, 'section')  26.6 us
    all_gather x1, blocking collectives, per_device(): piece_keys = lax.all_gather(key_rows, 'seq', axis=0, tiled=True)  20.5 us
    all_gather x1, blocking collectives, per_device(): piece_values = lax.all_gather(value_rows, 'seq', axis=0, tiled=True)  16.1 us
    all_gather x1, blocking collectives, per_device(): key_segs = lax.all_gather(seg_ids, 'seq', axis=0, tiled=True)  15.7 us
  transfers between devices with their start and end apart: 3, of which 3 were waited for; matrix products, arithmetic and copies ran while one was open for 0% of the time, Pallas kernels for 0%

commit v1 on v0

--- a/solution.py
+++ b/solution.py
@@ -60,7 +60,11 @@
     value_rows = jnp.dot(normed, w_value, preferred_element_type=jnp.float32).astype(jnp.bfloat16)
     score_scale = 1.0 / math.sqrt(head_dim)
     run_max = jnp.full((tok_seq,), -1e30, jnp.float32)
-    piece_keys = lax.all_gather(key_rows, "seq", axis=0, tiled=True)
+    peers = lax.axis_size("seq")
+    repeats = [peers if d == 0 else 1 for d in range(key_rows.ndim)]
+    piece_keys = lax.all_to_all(
+        jnp.tile(key_rows, repeats), "seq", split_axis=0, concat_axis=0, tiled=True
+    )
     piece_values = lax.all_gather(value_rows, "seq", axis=0, tiled=True)
     key_segs = lax.all_gather(seg_ids, "seq", axis=0, tiled=True)
     piece_rows = piece_keys.shape[0]

time: 377 us -> 365 us (0.968)
  blocking collectives: 115 us -> 98.1 us
  starting transfers between devices: 6.96 us -> 14.6 us
  waiting for transfers between devices: 204 us -> 199 us
    all_gather x1 -> x0, blocking collectives: 20.5 us -> none  [per_device(): piece_keys = lax.all_gather(key_rows, 'seq', axis=0, tiled=True)]
    all_to_all x0 -> x1, starting transfers between devices: none -> 7.57 us  [per_device(): lax.all_to_all(jnp.tile(key_rows, repeats), 'seq', split_axis=0, concat_a...]
    psum x1, waiting for transfers between devices: 128 us -> 123 us  [per_device(): summed = lax.psum(partial_value, ('section', 'exp'))]
  transfers between devices with their start and end apart: 3 -> 4, of which waited for: 3 -> 3; matrix products, arithmetic and copies ran while one was open for 0% -> 0% of each run, Pallas kernels for 0% -> 0%
where the time goes in v1:
time: 365 us; the launch traced here: 364 us
  waiting for transfers between devices  199 us (55%)
  blocking collectives  98.1 us (27%)
  matrix products  19.1 us (5%)
  starting transfers between devices  14.6 us (4%)
  between operations  13.7 us (4%)
  local copies, waits for them, and re-layouts  12 us (3%)
  other arithmetic  7.82 us (2%)
    psum x1, waiting for transfers between devices, per_device(): summed = lax.psum(partial_value, ('section', 'exp'))  123 us
    all_to_all x1, blocking collectives, per_device(): lax.all_to_all(doubled, ('seq', 'exp'), split_axis=0, concat_axis=0, tile...  63 us
    all_to_all x1, waiting for transfers between devices, per_device(): lax.all_to_all(jnp.dot(activated, down_halves[0], preferred_element_type=...  49.4 us
    psum x1, waiting for transfers between devices, per_device(): moe_total = lax.psum(moe_part, 'section')  26.6 us
    all_gather x1, blocking collectives, per_device(): key_segs = lax.all_gather(seg_ids, 'seq', axis=0, tiled=True)  18.6 us
    all_gather x1, blocking collectives, per_device(): piece_values = lax.all_gather(value_rows, 'seq', axis=0, tiled=True)  16.4 us
    all_to_all x1, starting transfers between devices, per_device(): lax.all_to_all(jnp.tile(key_rows, repeats), 'seq', split_axis=0, concat_a...  7.57 us
  transfers between devices with their start and end apart: 4, of which 3 were waited for; matrix products, arithmetic and copies ran while one was open for 0% of the time, Pallas kernels for 0%

profile of v1, /device:TPU:1, one launch (start us, length us, event | category | flops | bytes accessed | tf_op | source)
XLA Modules:
  0.0 364.1 jit_solution(2944089575382768795)
XLA Ops:
  6.5 1.3 fusion.4
  7.9 0.0 copy-start.5
  7.9 0.0 copy-start.2
  7.9 0.0 copy-start.8
  7.9 0.0 copy-start.9
  7.9 1.7 fusion.74
  9.6 1.6 fusion.76
  11.3 0.2 fusion.52
  11.5 0.1 copy.20
  11.6 0.9 tile.2
  12.5 7.6 %all-to-all-start = ((bf16[16,128,128]{2,1,0:T(8,128)(2,1)}), bf16[16,128,128]{2,1,0:T(8,128)(2,1)S(1)}, u32[]{:S(2)}, u32[]{:S(2)}) async-start(bf16[16,128,128]{2,1,0:T(8,128)(2,1)} %tile.2), calls=%async_computation | async-start | bytes 1048576 | tf_op jit(solution)/shard_map/all_to_all | solution.py:65
  20.1 0.0 all-reduce.3.cloned.1.call-start
  20.2 0.1 copy.22
  20.3 0.1 reshape.103
  20.4 18.6 %all-gather = s32[16,1,128]{2,1,0:T(1,128)S(1)} all-gather(s32[1,1,128]{2,1,0:T(1,128)S(1)} %bitcast.35), channel_id=1, replica_groups=mesh['section'=2,'seq'=16,'exp'=8] {'seq'}, dimensions={0}, use_global_device_ids=true | all-gather | bytes 8704 | tf_op jit(solution)/shard_map/all_gather | solution.py:69
  39.0 0.4 convolution_convert_fusion.2
  39.4 16.4 %all_gather.7 = bf16[2048,128]{1,0:T(8,128)(2,1)S(1)} all-gather(bf16[128,128]{1,0:T(8,128)(2,1)S(1)} %convolution_convert_fusion.2), channel_id=1, replica_groups=mesh['section'=2,'seq'=16,'exp'=8] {'seq'}, dimensions={0}, use_global_device_ids=true | all-gather | bytes 557056 | tf_op jit(solution)/shard_map/all_gather | solution.py:68
  55.8 0.8 copy-done.3
  56.6 1.6 fusion.78
  58.2 0.4 fusion.13
  58.6 2.8 fusion.3
  61.4 0.0 all-reduce.3.cloned.1.call-update
  61.4 0.1 fusion.42
  61.5 0.2 reduce_window_sum.11
  61.7 0.2 select_reduce_fusion
  61.9 122.9 %all-reduce.3.cloned.1.call-done = f32[128,2048]{1,0:T(8,128)} async-done(((f32[128,2048]{1,0:T(8,128)}), f32[128,2048]{1,0:T(8,128)}) %all-reduce.3.cloned.1.call-update) | async-done | bytes 1048592 | tf_op jit(solution)/shard_map/psum | solution.py:91
  184.7 1.0 fusion.35
  185.8 0.1 fusion.37
  185.9 0.5 convolution_convert_fusion.1
  186.4 0.4 broadcast_in_dim.19
  186.9 1.2 broadcast_in_dim.20
  188.1 63.0 %all_to_all.19 = bf16[128,4,2048]{2,1,0:T(4,128)(2,1)S(1)} all-to-all(bf16[128,4,2048]{2,1,0:T(4,128)(2,1)S(1)} %bitcast.30), channel_id=1, replica_groups=mesh['section'=2,'seq'=16,'exp'=8] {'seq','exp'}, dimensions={0} | all-to-all | bytes 4194304 | tf_op jit(solution)/shard_map/all_to_all | solution.py:121
  251.1 2.1 reshape.106
  253.2 3.5 fusion.10
  256.7 5.0 %convolution_convert_fusion = bf16[512,2048]{1,0:T(8,128)(2,1)} fusion(bf16[512,2048]{1,0:T(8,128)(2,1)S(1)} %copy-done.1, bf16[1,256,2048]{2,1,0:T(8,128)(2,1)S(1)} %copy-done, bf16[1,2048,256]{2,1,0:T(8,128)(2,1)} %param.24, f32[512,256]{1,0:T(8,128)} %fusion.10), kind=kOutput, calls=%fused_computation.1 | convolution fusion | flops 1075576832 | bytes 6815744 | tf_op jit(solution)/shard_map/dot_general | solution.py:127
  261.8 4.1 %reshape.107 = bf16[128,4,2048]{2,1,0:T(4,128)(2,1)} reshape(bf16[512,2048]{1,0:T(8,128)(2,1)} %convolution_convert_fusion) | data formatting | bytes 4194304 | tf_op jit(solution)/shard_map/reshape | solution.py:129
  265.9 6.7 %all-to-all-start.2 = ((bf16[128,4,2048]{2,1,0:T(4,128)(2,1)}), bf16[128,4,2048]{2,1,0:T(4,128)(2,1)S(1)}, u32[]{:S(2)}, u32[]{:S(2)}) async-start(bf16[128,4,2048]{2,1,0:T(4,128)(2,1)} %reshape.107), calls=%async_computation.2 | async-start | bytes 4194304 | tf_op jit(solution)/shard_map/all_to_all | solution.py:126
  272.6 0.2 all-reduce.5.cloned.1.call-start
  272.9 0.1 copy.21
  272.9 0.1 mul.147
  273.0 0.2 fusion.39
  273.2 49.4 %all-to-all-done.2 = bf16[128,4,2048]{2,1,0:T(4,128)(2,1)S(1)} async-done(((bf16[128,4,2048]{2,1,0:T(4,128)(2,1)}), bf16[128,4,2048]{2,1,0:T(4,128)(2,1)S(1)}, u32[]{:S(2)}, u32[]{:S(2)}) %all-to-all-start.2) | async-done | bytes 2097184 | tf_op jit(solution)/shard_map/all_to_all | solution.py:126
  322.6 2.7 convert_reduce_fusion
  325.3 2.0 reshape.108
  327.3 1.8 fusion.79
  329.0 0.0 all-reduce.5.cloned.1.call-update
  329.1 26.6 %all-reduce.5.cloned.1.call-done = f32[16,2048]{1,0:T(8,128)} async-done(((f32[16,2048]{1,0:T(8,128)}), f32[16,2048]{1,0:T(8,128)}) %all-reduce.5.cloned.1.call-update) | async-done | bytes 131088 | tf_op jit(solution)/shard_map/psum | solution.py:139
  355.7 1.5 fusion.38
  (25 shorter events, 0.1 us)
Async XLA Ops:
  6.5 250.2 %copy-start = (bf16[1,256,2048]{2,1,0:T(8,128)(2,1)S(1)}, bf16[1,256,2048]{2,1,0:T(8,128)(2,1)}, u32[]{:S(2)}) copy-start(bf16[1,256,2048]{2,1,0:T(8,128)(2,1)} %param.25) | copy-start | bytes 3145732
  7.9 12.3 %copy-start.6 = (s32[16,8]{0,1:T(8,128)S(1)}, s32[16,8]{0,1:T(8,128)}, u32[]{:S(2)}) copy-start(s32[16,8]{0,1:T(8,128)} %param.21) | copy-start | bytes 1540
  7.9 12.5 %copy-start.5 = (s32[128]{0:T(128)S(1)}, s32[128]{0:T(128)}, u32[]{:S(2)}) copy-start(s32[128]{0:T(128)} %param.14) | copy-start | bytes 1540
  7.9 31.1 %copy-start.2 = (bf16[128,2048]{1,0:T(8,128)(2,1)S(1)}, bf16[128,2048]{1,0:T(8,128)(2,1)}, u32[]{:S(2)}) copy-start(bf16[128,2048]{1,0:T(8,128)(2,1)} %param.13) | copy-start | bytes 1572868
  7.9 31.1 %copy-start.8 = (bf16[2048,128]{1,0:T(8,128)(2,1)S(1)}, bf16[2048,128]{1,0:T(8,128)(2,1)}, u32[]{:S(2)}) copy-start(bf16[2048,128]{1,0:T(8,128)(2,1)} %param.18) | copy-start | bytes 1572868
  7.9 31.1 %copy-start.9 = (f32[2048]{0:T(1024)S(1)}, f32[2048]{0:T(1024)}, u32[]{:S(2)}) copy-start(f32[2048]{0:T(1024)} %param.15) | copy-start | bytes 24580
  12.5 43.3 %all-to-all-start = ((bf16[16,128,128]{2,1,0:T(8,128)(2,1)}), bf16[16,128,128]{2,1,0:T(8,128)(2,1)S(1)}, u32[]{:S(2)}, u32[]{:S(2)}) async-start(bf16[16,128,128]{2,1,0:T(8,128)(2,1)} %tile.2), calls=%async_computation | async-start | bytes 1048576 | tf_op jit(solution)/shard_map/all_to_all | solution.py:65
  20.1 164.6 %all-reduce.3.cloned.1.call-start = ((), (), s32[]{:S(2)}) async-start(), calls=%async_computation.3 | async-start | bytes 2097152 | tf_op jit(solution)/shard_map/psum | solution.py:91
  55.8 0.8 copy-start.3
  58.6 127.2 %copy-start.4 = (f32[2048]{0:T(1024)S(1)}, f32[2048]{0:T(1024)}, u32[]{:S(2)}) copy-start(f32[2048]{0:T(1024)} %param.20) | copy-start | bytes 24580
  253.2 3.5 copy-start.1
  265.9 7.0 %copy-start.7 = (f32[16,8]{0,1:T(8,128)S(1)}, f32[16,8]{0,1:T(8,128)}, u32[]{:S(2)}) copy-start(f32[16,8]{0,1:T(8,128)} %param.22) | copy-start | bytes 1540
  265.9 56.7 %all-to-all-start.2 = ((bf16[128,4,2048]{2,1,0:T(4,128)(2,1)}), bf16[128,4,2048]{2,1,0:T(4,128)(2,1)S(1)}, u32[]{:S(2)}, u32[]{:S(2)}) async-start(bf16[128,4,2048]{2,1,0:T(4,128)(2,1)} %reshape.107), calls=%async_computation.2 | async-start | bytes 4194304 | tf_op jit(solution)/shard_map/all_to_all | solution.py:126
  272.6 83.1 %all-reduce.5.cloned.1.call-start = ((), (), s32[]{:S(2)}) async-start(), calls=%async_computation.4 | async-start | bytes 262144 | tf_op jit(solution)/shard_map/psum | solution.py:139
Sparse Core Ops, SparseCore 0:
  61.5 123.1 all-reduce.2
  329.2 26.4 all-reduce.4
